TPU v7x, 128 devices: a whole 4x4x4 slice. The times are simulated.
128 devices in a mesh: seq: 16 (over z, y), tp: 8 (over x, core).
Axes of the slice: x: 4, y: 4, z: 4, core: 2. Of those that a mesh axis runs over, the one named last changes fastest.
Arguments:
- tokens: bfloat16 [8192, 4096], P(('seq', 'tp')), may hold values from -24 to 24
- w_query: bfloat16 [4096, 4096], P(None, 'tp'), may hold values from -0.09375 to 0.09375
- w_key: bfloat16 [4096, 4096], P(None, 'tp'), may hold values from -0.09375 to 0.09375
- w_value: bfloat16 [4096, 4096], P(None, 'tp'), may hold values from -0.09375 to 0.09375
- w_out: bfloat16 [4096, 4096], P('tp'), may hold values from -0.09375 to 0.09375
- state_in: float32 [32, 128, 128], P('tp'), may hold values from -400 to 400
- grad_out: bfloat16 [8192, 4096], P(('seq', 'tp')), may hold values from -6 to 6
Outputs:
- mixed_out: bfloat16 [8192, 4096], P(('seq', 'tp'))
- input_grad: bfloat16 [8192, 4096], P(('seq', 'tp'))
- query_wgrad: float32 [4096, 4096], P('seq', 'tp')
- key_wgrad: float32 [4096, 4096], P('seq', 'tp')
- value_wgrad: float32 [4096, 4096], P('seq', 'tp')
- out_wgrad: float32 [4096, 4096], P('tp', 'seq')
- state_grad: float32 [32, 128, 128], P('tp', 'seq')
All inputs are finite; a program needn't handle non-finite values.
Results may differ from a plain program's by a relative error of at most 0.02.
Values may be sent and summed in bfloat16 or wider, within the bound.
No kernel may reach another device: no remote copies, remote signals or barrier semaphores. Data moves between devices by JAX's collectives and lax.ppermute only.
A program may use at most 128 MiB of HBM per device.

v0:
```python
import jax
import jax.numpy as jnp
from jax import lax
from jax.sharding import PartitionSpec as P

HIGH = lax.Precision.HIGHEST
ROWS_CONTRACT = (((0,), (0,)), ((), ()))
COLS_CONTRACT = (((1,), (1,)), ((), ()))


def scanned(array, axis):
    count = lax.axis_size(axis)
    place = lax.axis_index(axis)
    total = array
    before = jnp.zeros_like(array)
    after = jnp.zeros_like(array)
    step = 1
    while step < count:
        pairs = [(i, i ^ step) for i in range(count)]
        other = lax.ppermute(total, axis, pairs)
        upper = place & step != 0
        before = before + jnp.where(upper, other, 0.0)
        after = after + jnp.where(upper, 0.0, other)
        total = total + other
        step *= 2
    return (before, after, total)


def body(tokens, w_query, w_key, w_value, w_out, state_in, grad_out):
    head_count = state_in.shape[0]
    head_width = state_in.shape[1]
    rows_all = lax.all_gather(tokens, "tp", axis=0, tiled=True)
    shard_len = rows_all.shape[0]

    def head_split(matrix):
        return matrix.reshape(shard_len, head_count, head_width)

    query = jnp.dot(rows_all, w_query, preferred_element_type=jnp.float32).astype(jnp.bfloat16)
    key_all = jnp.dot(rows_all, w_key, preferred_element_type=jnp.float32).astype(jnp.bfloat16)
    value_all = jnp.dot(rows_all, w_value, preferred_element_type=jnp.float32).astype(jnp.bfloat16)
    query_heads = head_split(query)
    key_heads = head_split(key_all)
    value_heads = head_split(value_all)
    query_full = query_heads.astype(jnp.float32)
    key_full = key_heads.astype(jnp.float32)
    value_full = value_heads.astype(jnp.float32)
    local_kv = jnp.einsum(
        "thd,the->hde", key_heads, value_heads, preferred_element_type=jnp.float32
    )
    earlier, _, _ = scanned(local_kv, "seq")
    state_before = state_in + earlier
    row_ids = lax.broadcasted_iota(jnp.int32, (shard_len, shard_len), 0)
    col_ids = lax.broadcasted_iota(jnp.int32, (shard_len, shard_len), 1)
    mask = (row_ids >= col_ids)[None]
    scores = jnp.einsum("thd,shd->hts", query_heads, key_heads, preferred_element_type=jnp.float32)
    masked = jnp.where(mask, scores, 0.0)
    attn = jnp.einsum("hts,shd->thd", masked, value_full, precision=HIGH) + jnp.einsum(
        "thd,hde->the", query_full, state_before, precision=HIGH
    )
    inverse = lax.rsqrt(jnp.mean(attn * attn, axis=-1, keepdims=True) + 1e-05)
    normed = attn * inverse
    heads_out = normed.reshape(shard_len, head_count * head_width).astype(jnp.bfloat16)
    mixed_out = lax.psum_scatter(
        jnp.dot(heads_out, w_out, preferred_element_type=jnp.float32).astype(jnp.bfloat16),
        "tp",
        scatter_dimension=0,
        tiled=True,
    )
    grad_all = lax.all_gather(grad_out, "tp", axis=0, tiled=True)
    out_part = lax.dot_general(
        heads_out, grad_all, ROWS_CONTRACT, preferred_element_type=jnp.float32
    )
    d_normed = lax.dot_general(grad_all, w_out, COLS_CONTRACT, preferred_element_type=jnp.float32)
    d_normed = d_normed.reshape(shard_len, head_count, head_width)
    d_attn = inverse * (d_normed - normed * jnp.mean(d_normed * normed, axis=-1, keepdims=True))
    local_adj = jnp.einsum("thd,the->hde", query_full, d_attn, precision=HIGH)
    _, later, adj_total = scanned(local_adj, "seq")
    rows_per = head_width // lax.axis_size("seq")
    state_grad = lax.dynamic_slice_in_dim(
        adj_total, lax.axis_index("seq") * rows_per, rows_per, axis=1
    )
    mixed_s = jnp.where(mask, jnp.einsum("the,she->hts", d_attn, value_full, precision=HIGH), 0.0)
    grad_q = jnp.einsum("the,hde->thd", d_attn, state_before, precision=HIGH) + jnp.einsum(
        "hts,shd->thd", mixed_s, key_full, precision=HIGH
    )
    grad_k = jnp.einsum("hts,thd->shd", mixed_s, query_full, precision=HIGH) + jnp.einsum(
        "hde,she->shd", later, value_full, precision=HIGH
    )
    grad_v = jnp.einsum("hts,the->she", masked, d_attn, precision=HIGH) + jnp.einsum(
        "hde,shd->she", later, key_full, precision=HIGH
    )
    query_grad = grad_q.reshape(shard_len, head_count * head_width).astype(jnp.bfloat16)
    key_grad = grad_k.reshape(shard_len, head_count * head_width).astype(jnp.bfloat16)
    value_grad = grad_v.reshape(shard_len, head_count * head_width).astype(jnp.bfloat16)
    term = lax.dot_general(query_grad, w_query, COLS_CONTRACT, preferred_element_type=jnp.float32)
    term = term + lax.dot_general(
        key_grad, w_key, COLS_CONTRACT, preferred_element_type=jnp.float32
    )
    input_grad = lax.psum_scatter(
        (
            term
            + lax.dot_general(
                value_grad, w_value, COLS_CONTRACT, preferred_element_type=jnp.float32
            )
        ).astype(jnp.bfloat16),
        "tp",
        scatter_dimension=0,
        tiled=True,
    )
    query_part = lax.dot_general(
        rows_all, query_grad, ROWS_CONTRACT, preferred_element_type=jnp.float32
    )
    key_part = lax.dot_general(
        rows_all, key_grad, ROWS_CONTRACT, preferred_element_type=jnp.float32
    )
    value_part = lax.dot_general(
        rows_all, value_grad, ROWS_CONTRACT, preferred_element_type=jnp.float32
    )
    query_sum, key_sum, value_sum, out_summed = (
        lax.psum_scatter(
            query_part.astype(jnp.bfloat16), "seq", scatter_dimension=0, tiled=True
        ).astype(jnp.float32),
        lax.psum_scatter(
            key_part.astype(jnp.bfloat16), "seq", scatter_dimension=0, tiled=True
        ).astype(jnp.float32),
        lax.psum_scatter(
            value_part.astype(jnp.bfloat16), "seq", scatter_dimension=0, tiled=True
        ).astype(jnp.float32),
        lax.psum_scatter(
            out_part.astype(jnp.bfloat16), "seq", scatter_dimension=1, tiled=True
        ).astype(jnp.float32),
    )
    grad_scale = lax.rsqrt(jnp.float32(shard_len * lax.axis_size("seq")))
    return (
        mixed_out,
        input_grad,
        query_sum * grad_scale,
        key_sum * grad_scale,
        value_sum * grad_scale,
        out_summed * grad_scale,
        state_grad,
    )


def solution(mesh):
    return jax.shard_map(
        body,
        mesh=mesh,
        in_specs=(
            P(("seq", "tp"), None),
            P(None, "tp"),
            P(None, "tp"),
            P(None, "tp"),
            P("tp", None),
            P("tp", None, None),
            P(("seq", "tp"), None),
        ),
        out_specs=(
            P(("seq", "tp"), None),
            P(("seq", "tp"), None),
            P("seq", "tp"),
            P("seq", "tp"),
            P("seq", "tp"),
            P("tp", "seq"),
            P("tp", "seq", None),
        ),
        check_vma=False,
    )
```

profile of v0, /device:TPU:0, one launch (start us, length us, event | category | flops | bytes accessed | tf_op | source)
XLA Modules:
  0.0 514.8 jit_solution(3716976327167864774)
XLA Ops:
  7.2 0.7 all-gather.3.cloned.1.call-update
  7.9 0.7 all-gather.5.cloned.1.call-update
  8.7 35.6 %all-gather.3.cloned.1.call-done = bf16[512,4096]{1,0:T(8,128)(2,1)} async-done(((bf16[64,4096]{1,0:T(8,128)(2,1)}), bf16[512,4096]{1,0:T(8,128)(2,1)}) %all-gather.3.cloned.1.call-update) | async-done | bytes 4194320 | tf_op jit(solution)/shard_map/all_gather | solution.py:32
  44.3 6.0 %convolution_convert_fusion.5 = bf16[512,512]{0,1:T(8,128)(2,1)S(1)} fusion(bf16[512,4096]{1,0:T(8,128)(2,1)} %all-gather.3.cloned.1.call-done, bf16[4096,512]{1,0:T(8,128)(2,1)} %param.9), kind=kOutput, calls=%fused_computation.34 | convolution fusion | flops 2147745792 | bytes 8912896 | tf_op jit(solution)/shard_map/dot_general | solution.py:39
  50.3 2.4 convolution_convert_fusion.7
  52.7 0.3 fusion.36
  53.0 1.6 collective-permute-start
  54.6 6.9 %collective-permute-done = f32[4,128,128]{2,1,0:T(8,128)S(1)} collective-permute-done((f32[4,128,128]{2,1,0:T(8,128)S(1)}, f32[4,128,128]{2,1,0:T(8,128)S(1)}, u32[]{:S(2)}, u32[]{:S(2)}) %collective-permute-start) | collective-permute-done | bytes 262176 | tf_op jit(solution)/shard_map/ppermute | solution.py:20
  61.6 3.1 collective-permute-start.1
  64.6 6.0 %convolution_convert_fusion.6 = bf16[512,512]{0,1:T(8,128)(2,1)S(1)} fusion(bf16[512,4096]{1,0:T(8,128)(2,1)} %all-gather.3.cloned.1.call-done, bf16[4096,512]{1,0:T(8,128)(2,1)} %param.8), kind=kOutput, calls=%fused_computation.35 | convolution fusion | flops 2147745792 | bytes 8912896 | tf_op jit(solution)/shard_map/dot_general | solution.py:38
  70.6 0.3 collective-permute-done.1
  70.9 1.7 collective-permute-start.2
  72.6 0.7 fusion.35
  73.3 4.9 collective-permute-done.2
  78.3 3.4 collective-permute-start.3
  81.7 2.8 fusion.9
  84.5 2.0 collective-permute-done.3
  86.6 0.7 multiply_reduce_fusion.1
  87.4 5.9 %multiply_reduce_fusion = (f32[512,4]{0,1:T(4,128)S(1)}, f32[512,512]{0,1:T(8,128)S(1)}) fusion(f32[512,4,128]{0,2,1:T(8,128)S(1)} %get-tuple-element.17, f32[512,4]{0,1:T(4,128)S(1)} %add_rsqrt_fusion, bf16[512,4096]{1,0:T(8,128)(2,1)} %all-gather.5.cloned.1.call-done, bf16[512,4096]{1,0:T(8,128)(2,1)} %param.11), kind=kOutput, calls=%fused_computation.41 | convolution fusion | flops 2148268032 | bytes 10502144 | tf_op jit(solution)/shard_map/dot_general | solution.py:73
  93.3 1.1 subtract_multiply_fusion
  94.4 1.9 fusion.37
  96.3 2.8 fusion.5
  99.1 1.0 fusion.28
  100.1 0.8 copy-done.12
  100.9 4.6 fusion
  105.5 1.0 copy-done.10
  106.5 6.5 %convolution_convert_fusion = bf16[512,4096]{1,0:T(8,128)(2,1)} fusion(bf16[512,512]{0,1:T(8,128)(2,1)S(1)} %bitcast.92, bf16[512,4096]{1,0:T(8,128)(2,1)} %all-gather.5.cloned.1.call-done), kind=kOutput, calls=%fused_computation.1 | convolution fusion | flops 2149580800 | bytes 8912896 | tf_op jit(solution)/shard_map/dot_general | solution.py:70
  113.0 0.7 fusion.39
  113.7 1.2 collective-permute-start.4
  114.9 7.0 %collective-permute-done.4 = f32[4,128,128]{2,1,0:T(8,128)S(1)} collective-permute-done((f32[4,128,128]{2,1,0:T(8,128)S(1)}, f32[4,128,128]{2,1,0:T(8,128)S(1)}, u32[]{:S(2)}, u32[]{:S(2)}) %collective-permute-start.4) | collective-permute-done | bytes 262176 | tf_op jit(solution)/shard_map/ppermute | solution.py:20
  121.9 1.4 collective-permute-start.5
  123.3 8.7 %collective-permute-done.5 = f32[4,128,128]{2,1,0:T(8,128)S(1)} collective-permute-done((f32[4,128,128]{2,1,0:T(8,128)S(1)}, f32[4,128,128]{2,1,0:T(8,128)S(1)}, u32[]{:S(2)}, u32[]{:S(2)}) %collective-permute-start.5) | collective-permute-done | bytes 262176 | tf_op jit(solution)/shard_map/ppermute | solution.py:20
  132.0 2.2 collective-permute-start.6
  134.2 7.7 %collective-permute-done.6 = f32[4,128,128]{2,1,0:T(8,128)S(1)} collective-permute-done((f32[4,128,128]{2,1,0:T(8,128)S(1)}, f32[4,128,128]{2,1,0:T(8,128)S(1)}, u32[]{:S(2)}, u32[]{:S(2)}) %collective-permute-start.6) | collective-permute-done | bytes 262176 | tf_op jit(solution)/shard_map/ppermute | solution.py:20
  142.0 5.6 %collective-permute-start.7 = (f32[4,128,128]{2,1,0:T(8,128)S(1)}, f32[4,128,128]{2,1,0:T(8,128)S(1)}, u32[]{:S(2)}, u32[]{:S(2)}) collective-permute-start(f32[4,128,128]{2,1,0:T(8,128)S(1)} %add.106), channel_id=1, source_target_pairs={{0,64},{8,72},{16,80},{24,88},{32,96},{40,104},{48,112},{56,120},{... | collective-permute-start | bytes 786440 | tf_op jit(solution)/shard_map/ppermute | solution.py:20
  147.7 4.2 fusion.19
  151.8 1.6 collective-permute-done.7
  153.5 0.6 fusion.29
  154.2 4.3 fusion.1
  158.5 0.4 reduce-scatter.15.cloned.1.call-start
  159.0 5.2 %fusion.25 = f32[512,4,128]{0,2,1:T(8,128)S(1)} fusion(f32[512,4,128]{0,2,1:T(8,128)S(1)} %get-tuple-element.14, f32[4,512,512]{2,1,0:T(8,128)} %copy-done, pred[512,512]{1,0:T(8,128)(4,1)S(1)} %iota_compare_fusion), kind=kOutput, calls=%fused_computation.32 | convolution fusion | flops 1611661312 | bytes 6553600 | tf_op jit(solution)/shard_map/hts,the->she/dot_general | solution.py:89
  164.1 0.6 fusion.30
  164.8 0.8 copy-done.16
  165.6 4.4 fusion.2
  170.0 1.0 copy-done.11
  171.0 6.8 %convolution_convert_fusion.4 = bf16[512,4096]{1,0:T(8,128)(2,1)} fusion(bf16[512,512]{0,1:T(8,128)(2,1)S(1)} %bitcast.93, bf16[512,4096]{1,0:T(8,128)(2,1)} %param.11), kind=kOutput, calls=%fused_computation.5 | convolution fusion | flops 2149580800 | bytes 8912896 | tf_op jit(solution)/shard_map/dot_general | solution.py:64
  177.8 0.2 reduce-scatter.9.cloned.1.call-start
  178.0 0.8 copy-done.13
  178.8 4.7 fusion.38
  183.6 5.7 %fusion.40 = f32[512,4096]{1,0:T(8,128)} fusion(bf16[512,512]{0,1:T(8,128)(2,1)S(1)} %bitcast.97, bf16[4096,512]{1,0:T(8,128)(2,1)S(1)} %copy-done.5), kind=kOutput, calls=%fused_computation.63 | convolution fusion | flops 2147483648 | bytes 13107200 | tf_op jit(solution)/shard_map/dot_general | solution.py:96
  189.3 7.8 %add_convert_fusion = bf16[512,4096]{1,0:T(8,128)(2,1)} fusion(f32[512,4096]{1,0:T(8,128)S(1)} %fusion.38, f32[512,4096]{1,0:T(8,128)} %fusion.40, bf16[512,512]{0,1:T(8,128)(2,1)S(1)} %bitcast.99, bf16[4096,512]{1,0:T(8,128)(2,1)S(1)} %copy-done.7), kind=kOutput, calls=%fused_computation | convolution fusion | flops 2153775104 | bytes 25690112 | tf_op jit(solution)/shard_map/dot_general | solution.py:102
  197.1 1.3 dynamic-slice_add_fusion
  198.4 1.0 convert_multiply_fusion.3
  199.4 1.0 copy.26
  200.4 66.5 %reduce-scatter.17.cloned.1.call-done = bf16[512,256]{1,0:T(8,128)(2,1)} async-done(((bf16[512,4096]{1,0:T(8,128)(2,1)}), bf16[512,256]{1,0:T(8,128)(2,1)}) %reduce-scatter.17.cloned.1.call-update) | async-done | bytes 262160 | tf_op jit(solution)/shard_map/reduce_scatter | solution.py:129
  266.9 1.8 convert_multiply_fusion
  268.7 78.4 %reduce-scatter.13.cloned.1.call-done = bf16[256,512]{0,1:T(8,128)(2,1)} async-done(((bf16[4096,512]{0,1:T(8,128)(2,1)}), bf16[256,512]{0,1:T(8,128)(2,1)}) %reduce-scatter.13.cloned.1.call-update) | async-done | bytes 262160 | tf_op jit(solution)/shard_map/reduce_scatter | solution.py:123
  347.1 1.0 convert_multiply_fusion.2
  348.1 1.0 copy.27
  349.1 78.6 %reduce-scatter.15.cloned.1.call-done = bf16[256,512]{0,1:T(8,128)(2,1)} async-done(((bf16[4096,512]{0,1:T(8,128)(2,1)}), bf16[256,512]{0,1:T(8,128)(2,1)}) %reduce-scatter.15.cloned.1.call-update) | async-done | bytes 262160 | tf_op jit(solution)/shard_map/reduce_scatter | solution.py:126
  427.7 1.0 convert_multiply_fusion.1
  428.7 1.0 copy.28
  429.7 38.1 %reduce-scatter.7.cloned.1.call-done = bf16[64,4096]{1,0:T(8,128)(2,1)} async-done(((bf16[512,4096]{1,0:T(8,128)(2,1)}), bf16[64,4096]{1,0:T(8,128)(2,1)}) %reduce-scatter.7.cloned.1.call-update) | async-done | bytes 524304 | tf_op jit(solution)/shard_map/reduce_scatter | solution.py:63
  467.9 39.9 %reduce-scatter.9.cloned.1.call-done = bf16[64,4096]{1,0:T(8,128)(2,1)} async-done(((bf16[512,4096]{1,0:T(8,128)(2,1)}), bf16[64,4096]{1,0:T(8,128)(2,1)}) %reduce-scatter.9.cloned.1.call-update) | async-done | bytes 524304 | tf_op jit(solution)/shard_map/reduce_scatter | solution.py:99
  (70 shorter events, 0.9 us)
Async XLA Ops:
  7.2 37.1 %all-gather.3.cloned.1.call-start = ((), (), s32[]{:S(2)}) async-start(), calls=%async_computation.6 | async-start | bytes 4718592 | tf_op jit(solution)/shard_map/all_gather | solution.py:32
  7.9 79.5 %all-gather.5.cloned.1.call-start = ((), (), s32[]{:S(2)}) async-start(), calls=%async_computation.8 | async-start | bytes 4718592 | tf_op jit(solution)/shard_map/all_gather | solution.py:69
  8.6 189.8 %reduce-scatter.11.cloned.1.call-start = ((), (), s32[]{:S(2)}) async-start(), calls=%async_computation.10 | async-start | bytes 4456448 | tf_op jit(solution)/shard_map/reduce_scatter | solution.py:120
  44.3 6.0 %copy-start.6 = (bf16[4096,512]{1,0:T(8,128)(2,1)S(1)}, bf16[4096,512]{1,0:T(8,128)(2,1)}, u32[]{:S(2)}) copy-start(bf16[4096,512]{1,0:T(8,128)(2,1)} %param.10) | copy-start | bytes 12582916
  44.3 6.0 %copy-start.21 = (bf16[512,4096]{1,0:T(8,128)(2,1)S(1)}, bf16[512,4096]{1,0:T(8,128)(2,1)}, u32[]{:S(2)}) copy-start(bf16[512,4096]{1,0:T(8,128)(2,1)} %all-gather.3.cloned.1.call-done) | copy-start | bytes 12582916
  52.7 29.0 %copy-start.2 = (bf16[512,512]{0,1:T(8,128)(2,1)}, bf16[512,512]{0,1:T(8,128)(2,1)S(1)}, u32[]{:S(2)}) copy-start(bf16[512,512]{0,1:T(8,128)(2,1)S(1)} %convolution_convert_fusion.7) | copy-start | bytes 1572868
  53.0 8.5 %collective-permute-start = (f32[4,128,128]{2,1,0:T(8,128)S(1)}, f32[4,128,128]{2,1,0:T(8,128)S(1)}, u32[]{:S(2)}, u32[]{:S(2)}) collective-permute-start(f32[4,128,128]{2,1,0:T(8,128)S(1)} %fusion.36), channel_id=1, source_target_pairs={{0,8},{8,0},{16,24},{24,16},{32,40},{40,32},{48,56},{56,48},{64,72... | collective-permute-start | bytes 786440 | tf_op jit(solution)/shard_map/ppermute | solution.py:20
  61.6 9.3 %collective-permute-start.1 = (f32[4,128,128]{2,1,0:T(8,128)S(1)}, f32[4,128,128]{2,1,0:T(8,128)S(1)}, u32[]{:S(2)}, u32[]{:S(2)}) collective-permute-start(f32[4,128,128]{2,1,0:T(8,128)S(1)} %add.90), channel_id=1, source_target_pairs={{0,16},{8,24},{16,0},{24,8},{32,48},{40,56},{48,32},{56,40},{64,80... | collective-permute-start | bytes 786440 | tf_op jit(solution)/shard_map/ppermute | solution.py:20
  70.9 7.3 %collective-permute-start.2 = (f32[4,128,128]{2,1,0:T(8,128)S(1)}, f32[4,128,128]{2,1,0:T(8,128)S(1)}, u32[]{:S(2)}, u32[]{:S(2)}) collective-permute-start(f32[4,128,128]{2,1,0:T(8,128)S(1)} %add.92), channel_id=1, source_target_pairs={{0,32},{8,40},{16,48},{24,56},{32,0},{40,8},{48,16},{56,24},{64,96... | collective-permute-start | bytes 786440 | tf_op jit(solution)/shard_map/ppermute | solution.py:20
  73.3 13.3 %copy-start = (f32[4,512,512]{2,1,0:T(8,128)}, f32[4,512,512]{2,1,0:T(8,128)S(1)}, u32[]{:S(2)}) copy-start(f32[4,512,512]{2,1,0:T(8,128)S(1)} %fusion.35) | copy-start | bytes 12582916
  73.3 13.2 %copy-start.20 = (f32[4,128,128]{2,1,0:T(8,128)S(1)}, f32[4,128,128]{2,1,0:T(8,128)}, u32[]{:S(2)}) copy-start(f32[4,128,128]{2,1,0:T(8,128)} %param.12) | copy-start | bytes 786436
  78.3 8.2 %collective-permute-start.3 = (f32[4,128,128]{2,1,0:T(8,128)S(1)}, f32[4,128,128]{2,1,0:T(8,128)S(1)}, u32[]{:S(2)}, u32[]{:S(2)}) collective-permute-start(f32[4,128,128]{2,1,0:T(8,128)S(1)} %add.94), channel_id=1, source_target_pairs={{0,64},{8,72},{16,80},{24,88},{32,96},{40,104},{48,112},{56,120},{... | collective-permute-start | bytes 786440 | tf_op jit(solution)/shard_map/ppermute | solution.py:20
  86.6 0.7 copy-start.8
  87.4 7.0 %copy-start.3 = (bf16[512,512]{0,1:T(8,128)(2,1)S(1)}, bf16[512,512]{0,1:T(8,128)(2,1)}, u32[]{:S(2)}) copy-start(bf16[512,512]{0,1:T(8,128)(2,1)} %copy-done.2) | copy-start | bytes 1572868
  96.2 3.8 copy-start.1
  96.3 2.8 copy-start.9
  96.3 4.6 copy-start.22
  100.1 0.8 copy-start.12
  105.5 1.0 copy-start.10
  105.5 161.4 %reduce-scatter.17.cloned.1.call-start = ((), (), s32[]{:S(2)}) async-start(), calls=%async_computation.13 | async-start | bytes 4456448 | tf_op jit(solution)/shard_map/reduce_scatter | solution.py:129
  113.0 234.2 %reduce-scatter.13.cloned.1.call-start = ((), (), s32[]{:S(2)}) async-start(), calls=%async_computation.11 | async-start | bytes 4456448 | tf_op jit(solution)/shard_map/reduce_scatter | solution.py:123
  113.7 8.2 %collective-permute-start.4 = (f32[4,128,128]{2,1,0:T(8,128)S(1)}, f32[4,128,128]{2,1,0:T(8,128)S(1)}, u32[]{:S(2)}, u32[]{:S(2)}) collective-permute-start(f32[4,128,128]{2,1,0:T(8,128)S(1)} %fusion.39), channel_id=1, source_target_pairs={{0,8},{8,0},{16,24},{24,16},{32,40},{40,32},{48,56},{56,48},{64,72... | collective-permute-start | bytes 786440 | tf_op jit(solution)/shard_map/ppermute | solution.py:20
  121.9 10.1 %collective-permute-start.5 = (f32[4,128,128]{2,1,0:T(8,128)S(1)}, f32[4,128,128]{2,1,0:T(8,128)S(1)}, u32[]{:S(2)}, u32[]{:S(2)}) collective-permute-start(f32[4,128,128]{2,1,0:T(8,128)S(1)} %add.102), channel_id=1, source_target_pairs={{0,16},{8,24},{16,0},{24,8},{32,48},{40,56},{48,32},{56,40},{64,80... | collective-permute-start | bytes 786440 | tf_op jit(solution)/shard_map/ppermute | solution.py:20
  132.0 21.5 %copy-start.4 = (bf16[512,512]{0,1:T(8,128)(2,1)S(1)}, bf16[512,512]{0,1:T(8,128)(2,1)}, u32[]{:S(2)}) copy-start(bf16[512,512]{0,1:T(8,128)(2,1)} %copy-done.2) | copy-start | bytes 1572868
  132.0 9.9 %collective-permute-start.6 = (f32[4,128,128]{2,1,0:T(8,128)S(1)}, f32[4,128,128]{2,1,0:T(8,128)S(1)}, u32[]{:S(2)}, u32[]{:S(2)}) collective-permute-start(f32[4,128,128]{2,1,0:T(8,128)S(1)} %add.104), channel_id=1, source_target_pairs={{0,32},{8,40},{16,48},{24,56},{32,0},{40,8},{48,16},{56,24},{64,96... | collective-permute-start | bytes 786440 | tf_op jit(solution)/shard_map/ppermute | solution.py:20
  142.0 12.1 %copy-start.18 = (f32[4,128,128]{2,1,0:T(8,128)}, f32[4,128,128]{2,1,0:T(8,128)S(1)}, u32[]{:S(2)}) copy-start(f32[4,128,128]{2,1,0:T(8,128)S(1)} %add.106) | copy-start | bytes 786436
  142.0 12.2 %copy-start.23 = (bf16[512,4096]{1,0:T(8,128)(2,1)S(1)}, bf16[512,4096]{1,0:T(8,128)(2,1)}, u32[]{:S(2)}) copy-start(bf16[512,4096]{1,0:T(8,128)(2,1)} %all-gather.3.cloned.1.call-done) | copy-start | bytes 12582916
  142.0 11.4 %collective-permute-start.7 = (f32[4,128,128]{2,1,0:T(8,128)S(1)}, f32[4,128,128]{2,1,0:T(8,128)S(1)}, u32[]{:S(2)}, u32[]{:S(2)}) collective-permute-start(f32[4,128,128]{2,1,0:T(8,128)S(1)} %add.106), channel_id=1, source_target_pairs={{0,64},{8,72},{16,80},{24,88},{32,96},{40,104},{48,112},{56,120},{... | collective-permute-start | bytes 786440 | tf_op jit(solution)/shard_map/ppermute | solution.py:20
  153.4 0.7 copy-start.19
  154.2 4.3 copy-start.14
  158.5 269.2 %reduce-scatter.15.cloned.1.call-start = ((), (), s32[]{:S(2)}) async-start(), calls=%async_computation.12 | async-start | bytes 4456448 | tf_op jit(solution)/shard_map/reduce_scatter | solution.py:126
  159.0 6.6 %copy-start.24 = (bf16[512,4096]{1,0:T(8,128)(2,1)S(1)}, bf16[512,4096]{1,0:T(8,128)(2,1)}, u32[]{:S(2)}) copy-start(bf16[512,4096]{1,0:T(8,128)(2,1)} %all-gather.3.cloned.1.call-done) | copy-start | bytes 12582916
  164.8 0.8 copy-start.16
  169.9 1.0 copy-start.11
  170.0 297.9 %reduce-scatter.7.cloned.1.call-start = ((), (), s32[]{:S(2)}) async-start(), calls=%async_computation.7 | async-start | bytes 4718592 | tf_op jit(solution)/shard_map/reduce_scatter | solution.py:63
  177.7 1.1 copy-start.13
  177.8 5.8 %copy-start.15 = (bf16[512,4,128]{0,2,1:T(8,128)(2,1)S(1)}, bf16[512,4,128]{0,2,1:T(8,128)(2,1)}, u32[]{:S(2)}) copy-start(bf16[512,4,128]{0,2,1:T(8,128)(2,1)} %copy-done.14) | copy-start | bytes 1572868
  177.8 329.9 %reduce-scatter.9.cloned.1.call-start = ((), (), s32[]{:S(2)}) async-start(), calls=%async_computation.9 | async-start | bytes 4718592 | tf_op jit(solution)/shard_map/reduce_scatter | solution.py:99
  178.8 4.8 copy-start.5
  183.6 5.7 %copy-start.7 = (bf16[4096,512]{1,0:T(8,128)(2,1)S(1)}, bf16[4096,512]{1,0:T(8,128)(2,1)}, u32[]{:S(2)}) copy-start(bf16[4096,512]{1,0:T(8,128)(2,1)} %param.10) | copy-start | bytes 12582916
  183.6 5.7 %copy-start.17 = (bf16[512,4,128]{0,2,1:T(8,128)(2,1)S(1)}, bf16[512,4,128]{0,2,1:T(8,128)(2,1)}, u32[]{:S(2)}) copy-start(bf16[512,4,128]{0,2,1:T(8,128)(2,1)} %copy-done.16) | copy-start | bytes 1572868
Sparse Core Ops, SparseCore 0:
  9.7 34.5 all-gather.2
  46.0 32.0 all-gather.4
  105.6 80.6 reduce-scatter.10
  189.9 77.0 reduce-scatter.16
  270.1 77.0 reduce-scatter.12
  350.7 76.9 reduce-scatter.14
  430.7 37.1 reduce-scatter.6
  470.8 36.8 reduce-scatter.8
where the time goes:
time: 522 us; the launch traced here: 515 us
  waiting for transfers between devices  378 us (72%)
  matrix products  86.3 us (17%)
  starting transfers between devices  21 us (4%)
  between operations  14.8 us (3%)
  other arithmetic  7.62 us (1%)
  local copies, waits for them, and re-layouts  7.4 us (1%)
    reduce_scatter x1, waiting for transfers between devices, body(): lax.psum_scatter(value_part.astype(jnp.bfloat16), 'seq', scatter_dimensio...  78.6 us
    reduce_scatter x1, waiting for transfers between devices, body(): lax.psum_scatter(key_part.astype(jnp.bfloat16), 'seq', scatter_dimension=...  78.4 us
    reduce_scatter x1, waiting for transfers between devices, body(): lax.psum_scatter(out_part.astype(jnp.bfloat16), 'seq', scatter_dimension=...  66.5 us
    reduce_scatter x1, waiting for transfers between devices, body(): lax.psum_scatter((term + lax.dot_general(value_grad, w_value, COLS_CONTRA...  39.9 us
    ppermute x8, waiting for transfers between devices, scanned(): other = lax.ppermute(total, axis, pairs)  39.1 us
    reduce_scatter x1, waiting for transfers between devices, body(): lax.psum_scatter(jnp.dot(heads_out, w_out, preferred_element_type=jnp.flo...  38.1 us
    all_gather x1, waiting for transfers between devices, body(): rows_all = lax.all_gather(tokens, 'tp', axis=0, tiled=True)  35.6 us
    ppermute x8, starting transfers between devices, scanned(): other = lax.ppermute(total, axis, pairs)  20.1 us
  transfers between devices with their start and end apart: 16, of which 14 were waited for; matrix products, arithmetic and copies ran while one was open for 15% of the time, Pallas kernels for 0%

commit v1 on v0

--- a/solution.py
+++ b/solution.py
@@ -29,7 +29,9 @@
 def body(tokens, w_query, w_key, w_value, w_out, state_in, grad_out):
     head_count = state_in.shape[0]
     head_width = state_in.shape[1]
-    rows_all = lax.all_gather(tokens, "tp", axis=0, tiled=True)
+    rows_all = jnp.concatenate(
+        lax.all_to_all(jnp.stack([tokens] * lax.axis_size("tp")), "tp", 0, 0), axis=0
+    )
     shard_len = rows_all.shape[0]
 
     def head_split(matrix):

time: 522 us -> 565 us (1.082)
  waiting for transfers between devices: 378 us -> 401 us
  matrix products: 86.3 us -> 95.2 us
  starting transfers between devices: 21 us -> 28 us
    all_to_all x0 -> x1, waiting for transfers between devices: none -> 65.7 us  [body(): lax.all_to_all(jnp.stack([tokens] * lax.axis_size('tp')), 'tp', 0, 0)]
    all_gather x1 -> x0, waiting for transfers between devices: 35.6 us -> none  [body(): rows_all = lax.all_gather(tokens, 'tp', axis=0, tiled=True)]
    reduce_scatter x1, waiting for transfers between devices: 66.5 us -> 58.6 us  [body(): lax.psum_scatter(out_part.astype(jnp.bfloat16), 'seq', scatter_dimension=...]
  transfers between devices with their start and end apart: 16 -> 16, of which waited for: 14 -> 13; matrix products, arithmetic and copies ran while one was open for 15% -> 16% of each run, Pallas kernels for 0% -> 0%
where the time goes in v1:
time: 565 us; the launch traced here: 557 us
  waiting for transfers between devices  401 us (71%)
  matrix products  95.2 us (17%)
  starting transfers between devices  28 us (5%)
  between operations  14.7 us (3%)
  local copies, waits for them, and re-layouts  11 us (2%)
  other arithmetic  7.62 us (1%)
    reduce_scatter x1, waiting for transfers between devices, body(): lax.psum_scatter(value_part.astype(jnp.bfloat16), 'seq', scatter_dimensio...  78.6 us
    reduce_scatter x1, waiting for transfers between devices, body(): lax.psum_scatter(key_part.astype(jnp.bfloat16), 'seq', scatter_dimension=...  78.5 us
    all_to_all x1, waiting for transfers between devices, body(): lax.all_to_all(jnp.stack([tokens] * lax.axis_size('tp')), 'tp', 0, 0)  65.7 us
    reduce_scatter x1, waiting for transfers between devices, body(): lax.psum_scatter(out_part.astype(jnp.bfloat16), 'seq', scatter_dimension=...  58.6 us
    ppermute x8, waiting for transfers between devices, scanned(): other = lax.ppermute(total, axis, pairs)  40.7 us
    reduce_scatter x1, waiting for transfers between devices, body(): lax.psum_scatter((term + lax.dot_general(value_grad, w_value, COLS_CONTRA...  39.7 us
    reduce_scatter x1, waiting for transfers between devices, body(): lax.psum_scatter(jnp.dot(heads_out, w_out, preferred_element_type=jnp.flo...  38 us
    ppermute x8, starting transfers between devices, scanned(): other = lax.ppermute(total, axis, pairs)  22.6 us
  transfers between devices with their start and end apart: 16, of which 13 were waited for; matrix products, arithmetic and copies ran while one was open for 16% of the time, Pallas kernels for 0%

profile of v1, /device:TPU:0, one launch (start us, length us, event | category | flops | bytes accessed | tf_op | source)
XLA Modules:
  0.0 557.3 jit_solution(8156829097088839962)
XLA Ops:
  7.2 3.6 stack.2
  10.8 4.6 all-to-all-start
  15.4 0.7 all-gather.2.cloned.1.call-update
  16.1 65.7 %all-to-all-done = bf16[8,64,4096]{2,1,0:T(8,128)(2,1)} async-done(((bf16[8,64,4096]{2,1,0:T(8,128)(2,1)}), bf16[8,64,4096]{2,1,0:T(8,128)(2,1)}, u32[]{:S(2)}, u32[]{:S(2)}) %all-to-all-start) | async-done | bytes 4194336 | tf_op jit(solution)/shard_map/all_to_all | solution.py:33
  81.9 6.0 %convolution_convert_fusion.5 = bf16[512,512]{0,1:T(8,128)(2,1)S(1)} fusion(bf16[512,4096]{1,0:T(8,128)(2,1)} %bitcast, bf16[4096,512]{1,0:T(8,128)(2,1)} %param.9), kind=kOutput, calls=%fused_computation.34 | convolution fusion | flops 2147745792 | bytes 8912896 | tf_op jit(solution)/shard_map/dot_general | solution.py:41
  87.8 4.6 convolution_convert_fusion.7
  92.5 0.3 fusion.36
  92.8 1.7 collective-permute-start
  94.6 6.1 %collective-permute-done = f32[4,128,128]{2,1,0:T(8,128)S(1)} collective-permute-done((f32[4,128,128]{2,1,0:T(8,128)S(1)}, f32[4,128,128]{2,1,0:T(8,128)S(1)}, u32[]{:S(2)}, u32[]{:S(2)}) %collective-permute-start) | collective-permute-done | bytes 262176 | tf_op jit(solution)/shard_map/ppermute | solution.py:20
  100.7 3.4 collective-permute-start.1
  104.1 5.8 %convolution_convert_fusion.6 = bf16[512,512]{0,1:T(8,128)(2,1)S(1)} fusion(bf16[512,4096]{1,0:T(8,128)(2,1)} %bitcast, bf16[4096,512]{1,0:T(8,128)(2,1)} %param.8), kind=kOutput, calls=%fused_computation.35 | convolution fusion | flops 2147745792 | bytes 8912896 | tf_op jit(solution)/shard_map/dot_general | solution.py:40
  110.0 2.0 collective-permute-start.2
  112.0 0.7 fusion.35
  112.7 4.1 collective-permute-done.2
  116.9 4.0 collective-permute-start.3
  120.9 2.8 fusion.9
  123.7 2.1 collective-permute-done.3
  125.9 0.7 multiply_reduce_fusion.1
  126.7 5.9 %multiply_reduce_fusion = (f32[512,4]{0,1:T(4,128)S(1)}, f32[512,512]{0,1:T(8,128)S(1)}) fusion(f32[512,4,128]{0,2,1:T(8,128)S(1)} %get-tuple-element.17, f32[512,4]{0,1:T(4,128)S(1)} %add_rsqrt_fusion, bf16[512,4096]{1,0:T(8,128)(2,1)} %all-gather.2.cloned.1.call-done, bf16[512,4096]{1,0:T(8,128)(2,1)} %param.11), kind=kOutput, calls=%fused_computation.41 | convolution fusion | flops 2148268032 | bytes 10502144 | tf_op jit(solution)/shard_map/dot_general | solution.py:75
  132.6 1.1 subtract_multiply_fusion
  133.7 1.9 fusion.37
  135.6 2.8 fusion.5
  138.4 1.0 fusion.28
  139.4 0.8 copy-done.12
  140.2 6.8 %fusion = bf16[4096,512]{0,1:T(8,128)(2,1)} fusion(bf16[512,512]{0,1:T(8,128)(2,1)S(1)} %bitcast.95, bf16[512,4096]{1,0:T(8,128)(2,1)} %bitcast), kind=kOutput, calls=%fused_computation.6 | convolution fusion | flops 2149580800 | bytes 8912896 | tf_op jit(solution)/shard_map/dot_general | solution.py:112
  147.0 1.0 copy-done.10
  148.0 6.5 %convolution_convert_fusion = bf16[512,4096]{1,0:T(8,128)(2,1)} fusion(bf16[512,512]{0,1:T(8,128)(2,1)S(1)} %bitcast.93, bf16[512,4096]{1,0:T(8,128)(2,1)} %all-gather.2.cloned.1.call-done), kind=kOutput, calls=%fused_computation.1 | convolution fusion | flops 2149580800 | bytes 8912896 | tf_op jit(solution)/shard_map/dot_general | solution.py:72
  154.5 0.7 fusion.39
  155.2 0.8 collective-permute-start.4
  156.0 9.7 %collective-permute-done.4 = f32[4,128,128]{2,1,0:T(8,128)S(1)} collective-permute-done((f32[4,128,128]{2,1,0:T(8,128)S(1)}, f32[4,128,128]{2,1,0:T(8,128)S(1)}, u32[]{:S(2)}, u32[]{:S(2)}) %collective-permute-start.4) | collective-permute-done | bytes 262176 | tf_op jit(solution)/shard_map/ppermute | solution.py:20
  165.7 3.9 collective-permute-start.5
  169.6 6.3 %collective-permute-done.5 = f32[4,128,128]{2,1,0:T(8,128)S(1)} collective-permute-done((f32[4,128,128]{2,1,0:T(8,128)S(1)}, f32[4,128,128]{2,1,0:T(8,128)S(1)}, u32[]{:S(2)}, u32[]{:S(2)}) %collective-permute-start.5) | collective-permute-done | bytes 262176 | tf_op jit(solution)/shard_map/ppermute | solution.py:20
  176.0 3.7 collective-permute-start.6
  179.7 10.0 %collective-permute-done.6 = f32[4,128,128]{2,1,0:T(8,128)S(1)} collective-permute-done((f32[4,128,128]{2,1,0:T(8,128)S(1)}, f32[4,128,128]{2,1,0:T(8,128)S(1)}, u32[]{:S(2)}, u32[]{:S(2)}) %collective-permute-start.6) | collective-permute-done | bytes 262176 | tf_op jit(solution)/shard_map/ppermute | solution.py:20
  189.7 3.2 collective-permute-start.7
  192.9 4.2 fusion.19
  197.1 2.3 collective-permute-done.7
  199.6 0.6 fusion.29
  200.2 6.8 %fusion.1 = bf16[4096,512]{0,1:T(8,128)(2,1)} fusion(bf16[512,512]{0,1:T(8,128)(2,1)S(1)} %bitcast.97, bf16[512,4096]{1,0:T(8,128)(2,1)} %bitcast), kind=kOutput, calls=%fused_computation.7 | convolution fusion | flops 2149580800 | bytes 8912896 | tf_op jit(solution)/shard_map/dot_general | solution.py:115
  207.0 0.4 reduce-scatter.15.cloned.1.call-start
  207.4 5.0 fusion.25
  212.4 0.6 fusion.30
  213.1 0.8 copy-done.16
  213.8 6.7 %fusion.2 = bf16[4096,512]{0,1:T(8,128)(2,1)} fusion(bf16[512,512]{0,1:T(8,128)(2,1)S(1)} %bitcast.99, bf16[512,4096]{1,0:T(8,128)(2,1)} %bitcast), kind=kOutput, calls=%fused_computation.8 | convolution fusion | flops 2149580800 | bytes 8912896 | tf_op jit(solution)/shard_map/dot_general | solution.py:118
  220.7 1.0 copy-done.11
  221.6 6.6 %convolution_convert_fusion.4 = bf16[512,4096]{1,0:T(8,128)(2,1)} fusion(bf16[512,512]{0,1:T(8,128)(2,1)S(1)} %bitcast.94, bf16[512,4096]{1,0:T(8,128)(2,1)} %param.11), kind=kOutput, calls=%fused_computation.5 | convolution fusion | flops 2149580800 | bytes 8912896 | tf_op jit(solution)/shard_map/dot_general | solution.py:66
  228.2 0.2 reduce-scatter.9.cloned.1.call-start
  228.5 0.8 copy-done.13
  229.3 4.7 fusion.38
  234.0 5.7 %fusion.40 = f32[512,4096]{1,0:T(8,128)} fusion(bf16[512,512]{0,1:T(8,128)(2,1)S(1)} %bitcast.98, bf16[4096,512]{1,0:T(8,128)(2,1)S(1)} %copy-done.5), kind=kOutput, calls=%fused_computation.63 | convolution fusion | flops 2147483648 | bytes 13107200 | tf_op jit(solution)/shard_map/dot_general | solution.py:98
  239.7 8.0 %add_convert_fusion = bf16[512,4096]{1,0:T(8,128)(2,1)} fusion(f32[512,4096]{1,0:T(8,128)S(1)} %fusion.38, f32[512,4096]{1,0:T(8,128)} %fusion.40, bf16[512,512]{0,1:T(8,128)(2,1)S(1)} %bitcast.100, bf16[4096,512]{1,0:T(8,128)(2,1)S(1)} %copy-done.7), kind=kOutput, calls=%fused_computation | convolution fusion | flops 2153775104 | bytes 25690112 | tf_op jit(solution)/shard_map/dot_general | solution.py:104
  247.7 1.3 dynamic-slice_add_fusion
  249.1 1.0 convert_multiply_fusion.3
  250.1 1.0 copy.26
  251.1 58.6 %reduce-scatter.17.cloned.1.call-done = bf16[512,256]{1,0:T(8,128)(2,1)} async-done(((bf16[512,4096]{1,0:T(8,128)(2,1)}), bf16[512,256]{1,0:T(8,128)(2,1)}) %reduce-scatter.17.cloned.1.call-update) | async-done | bytes 262160 | tf_op jit(solution)/shard_map/reduce_scatter | solution.py:131
  309.7 1.8 convert_multiply_fusion
  311.5 78.5 %reduce-scatter.13.cloned.1.call-done = bf16[256,512]{0,1:T(8,128)(2,1)} async-done(((bf16[4096,512]{0,1:T(8,128)(2,1)}), bf16[256,512]{0,1:T(8,128)(2,1)}) %reduce-scatter.13.cloned.1.call-update) | async-done | bytes 262160 | tf_op jit(solution)/shard_map/reduce_scatter | solution.py:125
  390.0 1.0 convert_multiply_fusion.2
  391.0 1.0 copy.27
  392.0 78.6 %reduce-scatter.15.cloned.1.call-done = bf16[256,512]{0,1:T(8,128)(2,1)} async-done(((bf16[4096,512]{0,1:T(8,128)(2,1)}), bf16[256,512]{0,1:T(8,128)(2,1)}) %reduce-scatter.15.cloned.1.call-update) | async-done | bytes 262160 | tf_op jit(solution)/shard_map/reduce_scatter | solution.py:128
  470.5 1.0 convert_multiply_fusion.1
  471.5 1.0 copy.28
  472.5 38.0 %reduce-scatter.7.cloned.1.call-done = bf16[64,4096]{1,0:T(8,128)(2,1)} async-done(((bf16[512,4096]{1,0:T(8,128)(2,1)}), bf16[64,4096]{1,0:T(8,128)(2,1)}) %reduce-scatter.7.cloned.1.call-update) | async-done | bytes 524304 | tf_op jit(solution)/shard_map/reduce_scatter | solution.py:65
  510.6 39.7 %reduce-scatter.9.cloned.1.call-done = bf16[64,4096]{1,0:T(8,128)(2,1)} async-done(((bf16[512,4096]{1,0:T(8,128)(2,1)}), bf16[64,4096]{1,0:T(8,128)(2,1)}) %reduce-scatter.9.cloned.1.call-update) | async-done | bytes 524304 | tf_op jit(solution)/shard_map/reduce_scatter | solution.py:101
  (62 shorter events, 0.9 us)
Async XLA Ops:
  10.8 71.1 %all-to-all-start = ((bf16[8,64,4096]{2,1,0:T(8,128)(2,1)}), bf16[8,64,4096]{2,1,0:T(8,128)(2,1)}, u32[]{:S(2)}, u32[]{:S(2)}) async-start(bf16[8,64,4096]{2,1,0:T(8,128)(2,1)} %stack.2), calls=%async_computation | async-start | bytes 8388608 | tf_op jit(solution)/shard_map/all_to_all | solution.py:33
  15.3 111.3 %all-gather.2.cloned.1.call-start = ((), (), s32[]{:S(2)}) async-start(), calls=%async_computation.8 | async-start | bytes 4718592 | tf_op jit(solution)/shard_map/all_gather | solution.py:71
  16.1 233.0 %reduce-scatter.11.cloned.1.call-start = ((), (), s32[]{:S(2)}) async-start(), calls=%async_computation.10 | async-start | bytes 4456448 | tf_op jit(solution)/shard_map/reduce_scatter | solution.py:122
  81.8 6.0 %copy-start.6 = (bf16[4096,512]{1,0:T(8,128)(2,1)S(1)}, bf16[4096,512]{1,0:T(8,128)(2,1)}, u32[]{:S(2)}) copy-start(bf16[4096,512]{1,0:T(8,128)(2,1)} %param.10) | copy-start | bytes 12582916
  92.4 28.4 %copy-start.2 = (bf16[512,512]{0,1:T(8,128)(2,1)}, bf16[512,512]{0,1:T(8,128)(2,1)S(1)}, u32[]{:S(2)}) copy-start(bf16[512,512]{0,1:T(8,128)(2,1)S(1)} %convolution_convert_fusion.7) | copy-start | bytes 1572868
  92.8 7.9 %collective-permute-start = (f32[4,128,128]{2,1,0:T(8,128)S(1)}, f32[4,128,128]{2,1,0:T(8,128)S(1)}, u32[]{:S(2)}, u32[]{:S(2)}) collective-permute-start(f32[4,128,128]{2,1,0:T(8,128)S(1)} %fusion.36), channel_id=1, source_target_pairs={{0,8},{8,0},{16,24},{24,16},{32,40},{40,32},{48,56},{56,48},{64,72... | collective-permute-start | bytes 786440 | tf_op jit(solution)/shard_map/ppermute | solution.py:20
  100.7 9.2 %collective-permute-start.1 = (f32[4,128,128]{2,1,0:T(8,128)S(1)}, f32[4,128,128]{2,1,0:T(8,128)S(1)}, u32[]{:S(2)}, u32[]{:S(2)}) collective-permute-start(f32[4,128,128]{2,1,0:T(8,128)S(1)} %add.90), channel_id=1, source_target_pairs={{0,16},{8,24},{16,0},{24,8},{32,48},{40,56},{48,32},{56,40},{64,80... | collective-permute-start | bytes 786440 | tf_op jit(solution)/shard_map/ppermute | solution.py:20
  110.0 6.9 %collective-permute-start.2 = (f32[4,128,128]{2,1,0:T(8,128)S(1)}, f32[4,128,128]{2,1,0:T(8,128)S(1)}, u32[]{:S(2)}, u32[]{:S(2)}) collective-permute-start(f32[4,128,128]{2,1,0:T(8,128)S(1)} %add.92), channel_id=1, source_target_pairs={{0,32},{8,40},{16,48},{24,56},{32,0},{40,8},{48,16},{56,24},{64,96... | collective-permute-start | bytes 786440 | tf_op jit(solution)/shard_map/ppermute | solution.py:20
  112.7 13.2 %copy-start = (f32[4,512,512]{2,1,0:T(8,128)}, f32[4,512,512]{2,1,0:T(8,128)S(1)}, u32[]{:S(2)}) copy-start(f32[4,512,512]{2,1,0:T(8,128)S(1)} %fusion.35) | copy-start | bytes 12582916
  112.7 13.1 %copy-start.20 = (f32[4,128,128]{2,1,0:T(8,128)S(1)}, f32[4,128,128]{2,1,0:T(8,128)}, u32[]{:S(2)}) copy-start(f32[4,128,128]{2,1,0:T(8,128)} %param.12) | copy-start | bytes 786436
  116.9 8.9 %collective-permute-start.3 = (f32[4,128,128]{2,1,0:T(8,128)S(1)}, f32[4,128,128]{2,1,0:T(8,128)S(1)}, u32[]{:S(2)}, u32[]{:S(2)}) collective-permute-start(f32[4,128,128]{2,1,0:T(8,128)S(1)} %add.94), channel_id=1, source_target_pairs={{0,64},{8,72},{16,80},{24,88},{32,96},{40,104},{48,112},{56,120},{... | collective-permute-start | bytes 786440 | tf_op jit(solution)/shard_map/ppermute | solution.py:20
  125.9 0.7 copy-start.8
  126.7 7.0 %copy-start.3 = (bf16[512,512]{0,1:T(8,128)(2,1)S(1)}, bf16[512,512]{0,1:T(8,128)(2,1)}, u32[]{:S(2)}) copy-start(bf16[512,512]{0,1:T(8,128)(2,1)} %copy-done.2) | copy-start | bytes 1572868
  135.6 3.8 copy-start.1
  135.6 2.8 copy-start.9
  139.4 0.8 copy-start.12
  146.9 1.0 copy-start.10
  147.0 162.7 %reduce-scatter.17.cloned.1.call-start = ((), (), s32[]{:S(2)}) async-start(), calls=%async_computation.13 | async-start | bytes 4456448 | tf_op jit(solution)/shard_map/reduce_scatter | solution.py:131
  154.5 235.5 %reduce-scatter.13.cloned.1.call-start = ((), (), s32[]{:S(2)}) async-start(), calls=%async_computation.11 | async-start | bytes 4456448 | tf_op jit(solution)/shard_map/reduce_scatter | solution.py:125
  155.2 10.5 %collective-permute-start.4 = (f32[4,128,128]{2,1,0:T(8,128)S(1)}, f32[4,128,128]{2,1,0:T(8,128)S(1)}, u32[]{:S(2)}, u32[]{:S(2)}) collective-permute-start(f32[4,128,128]{2,1,0:T(8,128)S(1)} %fusion.39), channel_id=1, source_target_pairs={{0,8},{8,0},{16,24},{24,16},{32,40},{40,32},{48,56},{56,48},{64,72... | collective-permute-start | bytes 786440 | tf_op jit(solution)/shard_map/ppermute | solution.py:20
  165.7 10.2 %collective-permute-start.5 = (f32[4,128,128]{2,1,0:T(8,128)S(1)}, f32[4,128,128]{2,1,0:T(8,128)S(1)}, u32[]{:S(2)}, u32[]{:S(2)}) collective-permute-start(f32[4,128,128]{2,1,0:T(8,128)S(1)} %add.102), channel_id=1, source_target_pairs={{0,16},{8,24},{16,0},{24,8},{32,48},{40,56},{48,32},{56,40},{64,80... | collective-permute-start | bytes 786440 | tf_op jit(solution)/shard_map/ppermute | solution.py:20
  176.0 23.6 %copy-start.4 = (bf16[512,512]{0,1:T(8,128)(2,1)S(1)}, bf16[512,512]{0,1:T(8,128)(2,1)}, u32[]{:S(2)}) copy-start(bf16[512,512]{0,1:T(8,128)(2,1)} %copy-done.2) | copy-start | bytes 1572868
  176.0 13.7 %collective-permute-start.6 = (f32[4,128,128]{2,1,0:T(8,128)S(1)}, f32[4,128,128]{2,1,0:T(8,128)S(1)}, u32[]{:S(2)}, u32[]{:S(2)}) collective-permute-start(f32[4,128,128]{2,1,0:T(8,128)S(1)} %add.104), channel_id=1, source_target_pairs={{0,32},{8,40},{16,48},{24,56},{32,0},{40,8},{48,16},{56,24},{64,96... | collective-permute-start | bytes 786440 | tf_op jit(solution)/shard_map/ppermute | solution.py:20
  189.7 10.4 %copy-start.18 = (f32[4,128,128]{2,1,0:T(8,128)}, f32[4,128,128]{2,1,0:T(8,128)S(1)}, u32[]{:S(2)}) copy-start(f32[4,128,128]{2,1,0:T(8,128)S(1)} %add.106) | copy-start | bytes 786436
  189.7 9.7 %collective-permute-start.7 = (f32[4,128,128]{2,1,0:T(8,128)S(1)}, f32[4,128,128]{2,1,0:T(8,128)S(1)}, u32[]{:S(2)}, u32[]{:S(2)}) collective-permute-start(f32[4,128,128]{2,1,0:T(8,128)S(1)} %add.106), channel_id=1, source_target_pairs={{0,64},{8,72},{16,80},{24,88},{32,96},{40,104},{48,112},{56,120},{... | collective-permute-start | bytes 786440 | tf_op jit(solution)/shard_map/ppermute | solution.py:20
  199.5 0.7 copy-start.19
  200.2 6.8 %copy-start.14 = (bf16[512,4,128]{0,2,1:T(8,128)(2,1)}, bf16[512,4,128]{0,2,1:T(8,128)(2,1)S(1)}, u32[]{:S(2)}) copy-start(bf16[512,4,128]{0,2,1:T(8,128)(2,1)S(1)} %fusion.29) | copy-start | bytes 1572868
  207.0 263.6 %reduce-scatter.15.cloned.1.call-start = ((), (), s32[]{:S(2)}) async-start(), calls=%async_computation.12 | async-start | bytes 4456448 | tf_op jit(solution)/shard_map/reduce_scatter | solution.py:128
  213.1 0.8 copy-start.16
  220.6 1.1 copy-start.11
  220.6 290.0 %reduce-scatter.7.cloned.1.call-start = ((), (), s32[]{:S(2)}) async-start(), calls=%async_computation.7 | async-start | bytes 4718592 | tf_op jit(solution)/shard_map/reduce_scatter | solution.py:65
  228.2 1.1 copy-start.13
  228.2 5.8 %copy-start.15 = (bf16[512,4,128]{0,2,1:T(8,128)(2,1)S(1)}, bf16[512,4,128]{0,2,1:T(8,128)(2,1)}, u32[]{:S(2)}) copy-start(bf16[512,4,128]{0,2,1:T(8,128)(2,1)} %copy-done.14) | copy-start | bytes 1572868
  228.2 322.1 %reduce-scatter.9.cloned.1.call-start = ((), (), s32[]{:S(2)}) async-start(), calls=%async_computation.9 | async-start | bytes 4718592 | tf_op jit(solution)/shard_map/reduce_scatter | solution.py:101
  229.2 4.8 copy-start.5
  234.0 5.7 %copy-start.7 = (bf16[4096,512]{1,0:T(8,128)(2,1)S(1)}, bf16[4096,512]{1,0:T(8,128)(2,1)}, u32[]{:S(2)}) copy-start(bf16[4096,512]{1,0:T(8,128)(2,1)} %param.10) | copy-start | bytes 12582916
  234.0 5.7 %copy-start.17 = (bf16[512,4,128]{0,2,1:T(8,128)(2,1)S(1)}, bf16[512,4,128]{0,2,1:T(8,128)(2,1)}, u32[]{:S(2)}) copy-start(bf16[512,4,128]{0,2,1:T(8,128)(2,1)} %copy-done.16) | copy-start | bytes 1572868
Sparse Core Ops, SparseCore 0:
  17.9 53.2 all-gather.1
  147.1 81.8 reduce-scatter.10
  232.7 76.9 reduce-scatter.16
  312.9 77.0 reduce-scatter.12
  393.5 76.9 reduce-scatter.14
  473.4 37.1 reduce-scatter.6
  513.5 36.7 reduce-scatter.8
